TPU v7x, 32 devices: a whole 2x2x4 slice. The times are simulated.
32 devices in a mesh: row: 4 (over y, core), col: 8 (over z, x).
Axes of the slice: x: 2, y: 2, z: 4, core: 2. Of those that a mesh axis runs over, the one named last changes fastest.
Arguments:
- hess: bfloat16 [10, 4, 256, 5, 8, 256], P(None, 'row', None, None, 'col'), may hold values from -6 to 6
- coupling: float32 [32, 256, 2, 256], P(('row', 'col')), may hold values from -6 to 6
- dest_row: int32 [32, 256, 1], P(('row', 'col')), may hold values from 0 to 3, as said below
- local_row: int32 [32, 256], P(('row', 'col')), may hold values from 256 to 2559
- live: int32 [32], P(('row', 'col')), may hold values from 1 to 256, 6144 in all
- pattern: int32 [40, 40], replicated, may hold values 0 or 1
Outputs:
- factor: float32 [10, 4, 256, 5, 8, 256], P(None, 'row', None, None, 'col')
Inputs may be any that keep to these rules, and one draw needn't show every extreme that they name: `dest_row`: among one owner's 256 slots, used or not, one grid row is named exactly 64 times and no grid row more than 64 times. The first live[d] slots of owner d are used; the counts sum to 6144 and one owner uses all 256.
All inputs are finite; a program needn't handle non-finite values. No bound on the sum of `live` on one device may be relied on, other than what follows from the above.
Results may differ from a plain program's by a relative error of at most 0.0003.
Values sent between devices are 32-bit elements; how exact they have to be, the bound alone decides.
No kernel may reach another device: no remote copies, remote signals or barrier semaphores. Data moves between devices by JAX's collectives and lax.ppermute only.
A program may use at most 192 MiB of HBM per device.

v0:
```python
import jax
import jax.numpy as jnp
from jax import lax
from jax.sharding import PartitionSpec as P


def broadcast(value, axis, source):
    kept = jnp.where(lax.axis_index(axis) == source, value, 0).astype(value.dtype)
    return lax.psum(kept, axis)


def symmetric(block):
    return jnp.tril(block) + jnp.swapaxes(jnp.tril(block, -1), -1, -2)


def right_solve(rows, lower_factor):
    return jax.scipy.linalg.solve_triangular(lower_factor, rows.T, lower=True).T


def leading(block00, block10, block11, link):
    size = block00.shape[0]
    first = symmetric(block00)
    second = symmetric(block11)
    coupled = link * block10
    whole = jnp.concatenate(
        [jnp.concatenate([first, coupled.T], 1), jnp.concatenate([coupled, second], 1)], 0
    )
    ident = jnp.eye(2 * size, dtype=whole.dtype)
    spread = jnp.sum(jnp.abs(whole), axis=1) - jnp.abs(jnp.diagonal(whole))
    whole = whole * (1.0 - ident) + ident * (1.0 + spread)[:, None]
    factor00 = jnp.linalg.cholesky(whole[:size, :size])
    factor10 = right_solve(whole[size:, :size], factor00)
    reduced = whole[size:, size:] - jnp.dot(factor10, factor10.T, precision=lax.Precision.HIGHEST)
    factor11 = jnp.linalg.cholesky(reduced)
    return (factor00, factor10, factor11)


def solve_rows(rows, lower_factor):
    result = right_solve(rows, lower_factor)
    return result


def panel_solve(block_rows, f00, f10, f11):
    first = solve_rows(block_rows[:, 0], f00)
    second = solve_rows(
        block_rows[:, 1] - jnp.dot(first, f10.T, precision=lax.Precision.HIGHEST), f11
    )
    return jnp.stack([first, second], 1)


def shards(hess, coupling, dest_row, local_row, live, pattern):
    grid_rows = lax.axis_size("row")
    grid_cols = lax.axis_size("col")
    here_row = lax.axis_index("row")
    here_col = lax.axis_index("col")
    row_blocks = hess.shape[0]
    col_blocks = hess.shape[3]
    block = hess.shape[2]
    slot_count = coupling.shape[1]
    bucket = slot_count // 4
    height = row_blocks * block
    mask = pattern.astype(jnp.float32)
    grid_ids = jnp.arange(grid_rows, dtype=jnp.int32)
    dest = dest_row[0, :, 0]
    active = jnp.arange(slot_count, dtype=jnp.int32) < live[0]
    hits = (dest[:, None] == grid_ids[None, :]) & active[:, None]
    ranks = jnp.cumsum(hits.astype(jnp.int32), axis=0) - 1
    place = jnp.sum(jnp.where(hits, ranks + grid_ids[None, :] * bucket, 0), axis=1)
    place = jnp.where(active, place, grid_rows * bucket)
    outgoing = (
        jnp.zeros((grid_rows * bucket, 2, block), jnp.float32)
        .at[place]
        .set(coupling[0], mode="drop")
    )
    labels = (
        jnp.zeros((grid_rows * bucket,), jnp.float32)
        .at[place]
        .set(local_row[0].astype(jnp.float32), mode="drop")
    )
    arrived, arrived_rows = (
        lax.all_to_all(
            outgoing.reshape(grid_rows, bucket, 2, block),
            "row",
            split_axis=0,
            concat_axis=0,
            tiled=True,
        ),
        lax.all_to_all(
            labels.reshape(grid_rows, bucket), "row", split_axis=0, concat_axis=0, tiled=True
        ),
    )
    partial_value = (
        jnp.zeros((height, 2, block), jnp.float32)
        .at[arrived_rows.astype(jnp.int32).reshape(-1)]
        .add(arrived.reshape(-1, 2, block))
    )
    own = hess[:, 0, :, 0, 0, :].astype(jnp.float32).reshape(height, block)
    which = (jnp.arange(2, dtype=jnp.int32) == here_col).astype(jnp.float32)
    partial_value = partial_value + own[:, None, :] * which[None, :, None]
    corner = hess[0, 0, :, 0, 0, :].astype(jnp.float32)
    at_first = ((here_row == 0) & (here_col == 0)).astype(jnp.float32)
    at_below = ((here_row == 1) & (here_col == 0)).astype(jnp.float32)
    at_second = ((here_row == 1) & (here_col == 1)).astype(jnp.float32)
    pivots = lax.psum(
        jnp.stack([at_first * corner, at_below * corner, at_second * corner]), ("row", "col")
    )
    f00, f10, f11 = leading(pivots[0], pivots[1], pivots[2], mask[1, 0])
    mine = lax.dynamic_index_in_dim(
        mask.reshape(row_blocks, grid_rows, -1), here_row, 1, keepdims=False
    )
    rowmask = jnp.repeat(mine[:, :2], block, axis=0)
    summed = lax.psum(partial_value, "col")
    panel = panel_solve(summed * rowmask[:, :, None], f00, f10, f11)
    head_first = jnp.where(here_row == 0, f00, f10)
    head_second = jnp.where(here_row == 0, jnp.zeros_like(f11), f11)
    head = jnp.stack([head_first, head_second], 1)
    panel = panel.at[:block].set(jnp.where(here_row < 2, head, panel[:block]))
    ratio = grid_cols // grid_rows
    picked = lax.dynamic_index_in_dim(
        panel.reshape(col_blocks, ratio, block, 2, block), here_col // grid_rows, 1, keepdims=False
    )
    across = broadcast(picked, "row", here_col % grid_rows)
    left = panel.reshape(height, 2 * block)
    right = across.reshape(col_blocks * block, 2 * block)
    update = jnp.dot(left, right.T, precision=lax.Precision.HIGHEST).reshape(
        row_blocks, block, col_blocks, block
    )
    tiles = jnp.transpose(hess[:, 0, :, :, 0, :].astype(jnp.float32), (0, 2, 1, 3))
    sym = symmetric(tiles)
    block_i = jnp.arange(row_blocks, dtype=jnp.int32) * grid_rows + here_row
    block_j = jnp.arange(col_blocks, dtype=jnp.int32) * grid_cols + here_col
    links = lax.dynamic_index_in_dim(
        lax.dynamic_index_in_dim(
            mask.reshape(row_blocks, grid_rows, col_blocks, grid_cols), here_row, 1, keepdims=False
        ),
        here_col,
        2,
        keepdims=False,
    )
    same = (block_i[:, None] == block_j[None, :])[:, :, None, None]
    below = (block_i[:, None] > block_j[None, :])[:, :, None, None]
    base = jnp.where(same, sym, jnp.where(below, links[:, :, None, None] * tiles, 0.0))
    trail = base - jnp.transpose(update, (0, 2, 1, 3))
    lower_panel = jnp.transpose(panel.reshape(row_blocks, block, 2, block), (0, 2, 1, 3))
    panel_tile = lax.dynamic_index_in_dim(lower_panel, jnp.minimum(here_col, 1), 1, keepdims=False)
    in_panel = (block_j < 2)[None, :, None, None]
    kept = (block_i[:, None] >= block_j[None, :])[:, :, None, None]
    result = jnp.where(in_panel, panel_tile[:, None], jnp.where(kept, trail, 0.0))
    return jnp.transpose(result, (0, 2, 1, 3)).reshape(row_blocks, 1, block, col_blocks, 1, block)


def solution(mesh):
    return jax.shard_map(
        shards,
        mesh=mesh,
        in_specs=(
            P(None, "row", None, None, "col", None),
            P(("row", "col"), None, None, None),
            P(("row", "col"), None, None),
            P(("row", "col"), None),
            P(("row", "col")),
            P(),
        ),
        out_specs=P(None, "row", None, None, "col", None),
        check_vma=False,
    )
```

profile of v0, /device:TPU:0, one launch (start us, length us, event | category | flops | bytes accessed | tf_op | source)
XLA Modules:
  0.0 492.9 jit_solution(16189000699029080055)
XLA Ops:
  7.2 0.7 and_convert_fusion
  7.9 1.2 reduce-window.6
  9.5 0.7 convert_element_type.94
  10.2 0.8 fusion.47
  11.0 1.4 scatter_custom_fusion
  13.0 4.3 all-to-all-start
  17.2 1.0 fusion.18
  18.2 0.9 pad_maximum_fusion.3
  19.1 9.4 %copy.100 = bf16[10,1,256,5,1,256]{2,5,3,0,4,1:T(8,128)(2,1)} copy(bf16[10,1,256,5,1,256]{5,2,4,3,1,0:T(8,128)(2,1)} %param.11) | data formatting | bytes 13107200 | tf_op args[0]
  28.6 2.5 slice.121
  31.8 1.5 bitcast_convert_fusion
  33.5 4.2 broadcast_multiply_fusion.1
  37.9 0.8 copy.99
  38.7 0.9 broadcast_in_dim.117
  39.7 24.2 %scatter_fusion = f32[256,2,256]{2,1,0:T(2,128)} fusion(f32[256,2,256]{2,1,0:T(2,128)} %broadcast_in_dim.117, s32[256]{0:T(256)S(1)} %bitcast.222, f32[256,2,256]{2,1,0:T(2,128)S(1)} %bitcast.212), kind=kCustom, calls=%fused_computation.2 | custom fusion | bytes 1573888 | tf_op jit(solution)/shard_map/scatter | solution.py:73
  63.8 3.5 all-to-all-start.1
  67.5 8.7 %all-to-all-done.1 = f32[4,64,2,256]{3,2,1,0:T(2,128)S(1)} async-done(((f32[4,64,2,256]{3,2,1,0:T(2,128)}), f32[4,64,2,256]{3,2,1,0:T(2,128)S(1)}, u32[]{:S(2)}, u32[]{:S(2)}) %all-to-all-start.1) | async-done | bytes 524320 | tf_op jit(solution)/shard_map/all_to_all | solution.py:81
  76.2 30.9 %scatter_fusion.1 = f32[2560,2,256]{2,1,0:T(2,128)} fusion(f32[2560,2,256]{2,1,0:T(2,128)} %broadcast_multiply_fusion.1, s32[256]{0:T(256)S(1)} %bitcast.223, f32[256,2,256]{2,1,0:T(2,128)S(1)} %bitcast.211), kind=kCustom, calls=%fused_computation.3 | custom fusion | flops 131072 | bytes 1573888 | tf_op jit(solution)/shard_map/scatter-add | solution.py:95
  107.1 8.8 %copy.88 = f32[2560,2,256]{0,2,1:T(8,128)} copy(f32[2560,2,256]{2,1,0:T(2,128)} %scatter_fusion.1) | data formatting | bytes 10485760 | tf_op jit(solution)/shard_map/scatter-add | solution.py:95
  116.1 39.1 %all-reduce.5.cloned.1.call-done = f32[3,256,256]{2,1,0:T(8,128)} async-done(((f32[3,256,256]{2,1,0:T(8,128)}), f32[3,256,256]{2,1,0:T(8,128)}) %all-reduce.5.cloned.1.call-update) | async-done | bytes 786448 | tf_op jit(solution)/shard_map/psum | solution.py:104
  155.2 1.1 fusion.26
  156.6 1.7 fusion.29
  158.8 4.5 gather_fusion
  163.8 11.7 %cholesky.130 = f32[128,128]{1,0:T(8,128)S(1)} custom-call(f32[128,128]{1,0:T(8,128)S(1)} %cholesky.194), custom_call_target="Cholesky" | custom-call | tf_op jit(solution)/shard_map/jit(cholesky)/cholesky | solution.py:31
  175.5 9.8 %custom-call.20 = f32[1,128,128]{1,2,0:T(8,128)S(1)} custom-call(f32[1,128,128]{2,1,0:T(8,128)S(1)} %get-tuple-element.87), custom_call_target="InvertDiagBlocksLowerTriangular" | custom-call | tf_op jit(solution)/shard_map/jit(cholesky)/cholesky | solution.py:31
  185.8 11.7 %cholesky.147 = f32[128,128]{1,0:T(8,128)S(1)} custom-call(f32[128,128]{1,0:T(8,128)S(1)} %convolution_subtract_fusion.6), custom_call_target="Cholesky" | custom-call | tf_op jit(solution)/shard_map/jit(cholesky)/cholesky | solution.py:31
  199.6 3.8 while.6
  200.2 1.3 bitcast_dynamic-update-slice_fusion.4
  202.1 1.3 bitcast_dynamic-update-slice_fusion.4
  203.4 20.1 %custom-call.21 = f32[2,128,128]{1,2,0:T(8,128)S(1)} custom-call(f32[2,128,128]{2,1,0:T(8,128)S(1)} %get-tuple-element.41), custom_call_target="InvertDiagBlocksLowerTriangular" | custom-call | tf_op jit(solution)/shard_map/jit(_solve_triangular)/triangular_solve | solution.py:17
  225.2 11.7 %cholesky.164 = f32[128,128]{1,0:T(8,128)S(1)} custom-call(f32[128,128]{1,0:T(8,128)S(1)} %cholesky.197), custom_call_target="Cholesky" | custom-call | tf_op jit(solution)/shard_map/jit(cholesky)/cholesky | solution.py:34
  237.0 9.8 %custom-call.22 = f32[1,128,128]{1,2,0:T(8,128)S(1)} custom-call(f32[1,128,128]{2,1,0:T(8,128)S(1)} %get-tuple-element.83), custom_call_target="InvertDiagBlocksLowerTriangular" | custom-call | tf_op jit(solution)/shard_map/jit(cholesky)/cholesky | solution.py:34
  247.3 11.7 %cholesky.181 = f32[128,128]{1,0:T(8,128)S(1)} custom-call(f32[128,128]{1,0:T(8,128)S(1)} %convolution_subtract_fusion.5), custom_call_target="Cholesky" | custom-call | tf_op jit(solution)/shard_map/jit(cholesky)/cholesky | solution.py:34
  261.5 0.8 select_bitcast_fusion
  262.3 3.8 while.7
  262.9 1.3 bitcast_dynamic-update-slice_fusion.5
  264.8 1.3 bitcast_dynamic-update-slice_fusion.5
  266.1 20.5 %custom-call.23 = f32[2,128,128]{1,2,0:T(8,128)} custom-call(f32[2,128,128]{2,1,0:T(8,128)S(1)} %get-tuple-element.42), custom_call_target="InvertDiagBlocksLowerTriangular" | custom-call | tf_op jit(solution)/shard_map/jit(_solve_triangular)/triangular_solve | solution.py:17
  286.6 0.7 fusion.21
  287.3 54.9 %all-reduce.7.cloned.1.call-done = f32[2560,2,256]{0,2,1:T(8,128)} async-done(((f32[2560,2,256]{0,2,1:T(8,128)}), f32[2560,2,256]{0,2,1:T(8,128)}) %all-reduce.7.cloned.1.call-update) | async-done | bytes 5242896 | tf_op jit(solution)/shard_map/psum | solution.py:112
  342.2 3.0 broadcast_multiply_fusion
  345.4 2.2 copy-done.1
  347.6 1.3 fusion.13
  348.8 2.3 convolution_subtract_fusion.2
  351.6 3.5 fusion.42
  355.1 4.4 fusion.8
  359.6 1.3 fusion.11
  360.8 1.1 copy-done.2
  361.9 2.3 convolution_subtract_fusion.1
  364.2 2.8 copy.97
  367.2 1.1 copy-done.4
  368.4 2.4 fusion.34
  372.3 2.2 copy-done
  374.5 2.0 copy.107
  376.5 3.2 dot_general.16
  379.8 0.8 copy-done.9
  380.6 11.4 %convert_multiply_fusion = (f32[10,256,5,256]{1,3,2,0:T(8,128)}, f32[10,256,5,256]{1,3,2,0:T(8,128)}) fusion(bf16[10,1,256,5,1,256]{2,5,3,0,4,1:T(8,128)(2,1)} %copy.100, f32[10,5]{1,0:T(8,128)S(1)} %bitcast.215, pred[256,256]{0,1:T(8,128)(4,1)S(1)} %copy-done.9), kind=kLoop, calls=%fused_computation.8 | loop fusion | flops 9830400 | bytes 32833736 | tf_op jit(solution)/shard_map/mul | solution.py:142
  392.0 14.0 %copy.102 = f32[10,256,5,256]{3,1,2,0:T(8,128)} copy(f32[10,256,5,256]{1,3,2,0:T(8,128)} %get-tuple-element.67) | data formatting | bytes 26214400 | tf_op jit(solution)/shard_map/jit(tril)/select_n | solution.py:13
  406.0 14.1 %copy.105 = f32[10,256,5,256]{3,1,2,0:T(8,128)} copy(f32[10,256,5,256]{1,3,2,0:T(8,128)} %get-tuple-element.66) | data formatting | bytes 26214400 | tf_op jit(solution)/shard_map/mul | solution.py:142
  420.3 10.4 %copy.106 = f32[2560,2,256]{2,1,0:T(2,128)} copy(f32[2560,2,256]{2,0,1:T(8,128)} %copy-done) | data formatting | bytes 10485760 | tf_op jit(solution)/shard_map/scatter | solution.py:117
  430.7 8.0 %reshape.409 = f32[10,256,512,1]{2,1,0,3:T(8,128)} reshape(f32[2560,2,256]{2,1,0:T(2,128)} %copy.106) | data formatting | bytes 10485760 | tf_op jit(solution)/shard_map/dot_general | solution.py:125
  438.7 2.0 dynamic-slice_bitcast_fusion
  440.8 30.4 %fusion.6 = f32[10,1,256,5,1,256]{5,2,3,0,4,1:T(8,128)S(1)} fusion(f32[10,256,5,256]{3,1,2,0:T(8,128)} %copy.102, f32[10,256,5,256]{3,1,2,0:T(8,128)} %copy.105, bf16[10,1,256,5,1,256]{2,5,3,0,4,1:T(8,128)(2,1)} %copy.100, f32[10,256,256]{2,1,0:T(8,128)S(1)} %dynamic-slice_bitcast_fusion, pred[5]{0:T(512)(128)(4,1)S(1)} %broadcast_compare_fusion.3, ...), kind=kOutput, calls=%fused_computation.17 | convolution fusion | flops 20158873600 | bytes 56426652 | tf_op jit(solution)/shard_map/dot_general | solution.py:125
  471.2 15.0 %copy.108 = f32[10,1,256,5,1,256]{5,4,3,2,1,0:T(1,128)} copy(f32[10,1,256,5,1,256]{5,2,3,0,4,1:T(8,128)S(1)} %fusion.6) | data formatting | bytes 26214400 | tf_op jit(solution)/shard_map/reshape | solution.py:149
  (112 shorter events, 13.2 us)
Async XLA Ops:
  13.0 50.9 %all-to-all-start = ((f32[4,1,64]{2,1,0:T(1,128)}), f32[4,1,64]{2,1,0:T(1,128)S(1)}, u32[]{:S(2)}, u32[]{:S(2)}) async-start(f32[4,1,64]{2,1,0:T(1,128)} %all_to_all.9), calls=%async_computation | async-start | bytes 4096 | tf_op jit(solution)/shard_map/all_to_all | solution.py:88
  17.2 138.0 %all-reduce.5.cloned.1.call-start = ((), (), s32[]{:S(2)}) async-start(), calls=%async_computation.2 | async-start | bytes 1572864 | tf_op jit(solution)/shard_map/psum | solution.py:104
  28.6 2.5 copy-start.11
  33.5 6.2 %copy-start.8 = (f32[1,256,2,256]{3,2,1,0:T(2,128)S(1)}, f32[1,256,2,256]{3,2,1,0:T(2,128)}, u32[]{:S(2)}) copy-start(f32[1,256,2,256]{3,2,1,0:T(2,128)} %param.12) | copy-start | bytes 1572868
  63.8 12.3 %all-to-all-start.1 = ((f32[4,64,2,256]{3,2,1,0:T(2,128)}), f32[4,64,2,256]{3,2,1,0:T(2,128)S(1)}, u32[]{:S(2)}, u32[]{:S(2)}) async-start(f32[4,64,2,256]{3,2,1,0:T(2,128)} %bitcast.26), calls=%async_computation.1 | async-start | bytes 1048576 | tf_op jit(solution)/shard_map/all_to_all | solution.py:81
  67.4 274.8 %all-reduce.7.cloned.1.call-start = ((), (), s32[]{:S(2)}) async-start(), calls=%async_computation.3 | async-start | bytes 10485760 | tf_op jit(solution)/shard_map/psum | solution.py:112
  115.9 324.9 %all-reduce.9.cloned.1.call-start = ((), (), s32[]{:S(2)}) async-start(), calls=%async_computation.4 | async-start | bytes 5242880 | tf_op jit(solution)/shard_map/psum | solution.py:9
  155.2 3.2 copy-start.5
  345.2 2.4 copy-start.1
  355.1 4.4 copy-start.10
  360.8 1.1 copy-start.2
  367.0 1.3 copy-start.4
  368.4 2.4 copy-start.3
  371.0 1.0 copy-start.6
  371.0 1.0 copy-start.7
  372.1 2.4 copy-start
  379.7 0.8 copy-start.9
Sparse Core Ops, SparseCore 0:
  23.2 131.9 all-reduce.4
  158.9 183.2 all-reduce.6
  379.9 58.9 all-reduce.8
where the time goes:
time: 500 us; the launch traced here: 493 us
  other arithmetic  172 us (34%)
  local copies, waits for them, and re-layouts  143 us (29%)
  waiting for transfers between devices  103 us (21%)
  matrix products  50.3 us (10%)
  between operations  17 us (3%)
  starting transfers between devices  8.02 us (2%)
    psum x1, waiting for transfers between devices, shards(): summed = lax.psum(partial_value, 'col')  54.9 us
    another operation x5, other arithmetic, right_solve(): return jax.scipy.linalg.solve_triangular(lower_factor, rows.T, lower=True).T  40.6 us
    psum x1, waiting for transfers between devices, shards(): lax.psum(jnp.stack([at_first * corner, at_below * corner, at_second * cor...  39.1 us
    another operation x7, other arithmetic, leading(): factor11 = jnp.linalg.cholesky(reduced)  34.6 us
    another operation x6, other arithmetic, leading(): factor00 = jnp.linalg.cholesky(whole[:size, :size])  33.9 us
    scatter-add x1, other arithmetic, shards(): partial_value = jnp.zeros((height, 2, block), jnp.float32).at[arrived_row...  30.9 us
    dot_general x1, matrix products, shards(): jnp.dot(left, right.T, precision=lax.Precision.HIGHEST)  30.4 us
    scatter x1, local copies, waits for them, and re-layouts, shards(): outgoing = jnp.zeros((grid_rows * bucket, 2, block), jnp.float32).at[plac...  24.2 us
  transfers between devices with their start and end apart: 5, of which 3 were waited for; matrix products, arithmetic and copies ran while one was open for 56% of the time, Pallas kernels for 0%

commit v1 on v0

--- a/solution.py
+++ b/solution.py
@@ -101,8 +101,11 @@
     at_first = ((here_row == 0) & (here_col == 0)).astype(jnp.float32)
     at_below = ((here_row == 1) & (here_col == 0)).astype(jnp.float32)
     at_second = ((here_row == 1) & (here_col == 1)).astype(jnp.float32)
-    pivots = lax.psum(
-        jnp.stack([at_first * corner, at_below * corner, at_second * corner]), ("row", "col")
+    pivots = jnp.sum(
+        lax.all_gather(
+            jnp.stack([at_first * corner, at_below * corner, at_second * corner]), ("row", "col")
+        ),
+        axis=0,
     )
     f00, f10, f11 = leading(pivots[0], pivots[1], pivots[2], mask[1, 0])
     mine = lax.dynamic_index_in_dim(

time: 500 us -> 677 us (1.35)
  waiting for transfers between devices: 103 us -> 263 us
    psum x1, waiting for transfers between devices: 54.9 us -> 258 us  [shards(): summed = lax.psum(partial_value, 'col')]
    psum x1 -> x0, waiting for transfers between devices: 39.1 us -> none  [shards(): lax.psum(jnp.stack([at_first * corner, at_below * corner, at_second * cor...]
    reduce_sum x0 -> x1, other arithmetic: none -> 9.24 us  [shards(): jnp.sum(lax.all_gather(jnp.stack([at_first * corner, at_below * corner, a...]
    unnamed x28 -> x30, local copies, waits for them, and re-layouts: 17.6 us -> 16.9 us
  transfers between devices with their start and end apart: 5 -> 5, of which waited for: 3 -> 2; matrix products, arithmetic and copies ran while one was open for 56% -> 16% of each run, Pallas kernels for 0% -> 0%
where the time goes in v1:
time: 677 us; the launch traced here: 669 us
  waiting for transfers between devices  263 us (39%)
  other arithmetic  177 us (26%)
  local copies, waits for them, and re-layouts  145 us (21%)
  matrix products  56.9 us (8%)
  between operations  19.1 us (3%)
  starting transfers between devices  7.88 us (1%)
    psum x1, waiting for transfers between devices, shards(): summed = lax.psum(partial_value, 'col')  258 us
    another operation x5, other arithmetic, right_solve(): return jax.scipy.linalg.solve_triangular(lower_factor, rows.T, lower=True).T  40.6 us
    another operation x7, other arithmetic, leading(): factor11 = jnp.linalg.cholesky(reduced)  34.7 us
    another operation x6, other arithmetic, leading(): factor00 = jnp.linalg.cholesky(whole[:size, :size])  34 us
    scatter-add x1, other arithmetic, shards(): partial_value = jnp.zeros((height, 2, block), jnp.float32).at[arrived_row...  30.9 us
    dot_general x1, matrix products, shards(): jnp.dot(left, right.T, precision=lax.Precision.HIGHEST)  30.2 us
    scatter x1, local copies, waits for them, and re-layouts, shards(): outgoing = jnp.zeros((grid_rows * bucket, 2, block), jnp.float32).at[plac...  24.2 us
    another operation x9, matrix products, right_solve(): return jax.scipy.linalg.solve_triangular(lower_factor, rows.T, lower=True).T  17 us
  transfers between devices with their start and end apart: 5, of which 2 were waited for; matrix products, arithmetic and copies ran while one was open for 16% of the time, Pallas kernels for 0%

profile of v1, /device:TPU:0, one launch (start us, length us, event | category | flops | bytes accessed | tf_op | source)
XLA Modules:
  0.0 668.6 jit_solution(15550777185528799908)
XLA Ops:
  8.7 1.2 reduce-window.6
  11.0 0.8 fusion.47
  11.8 1.4 scatter_custom_fusion
  13.8 4.3 all-to-all-start
  18.1 1.3 slice-done
  19.7 0.9 broadcast_in_dim.117
  20.7 24.2 %scatter_fusion = f32[256,2,256]{2,1,0:T(2,128)} fusion(f32[256,2,256]{2,1,0:T(2,128)} %broadcast_in_dim.117, s32[256]{0:T(256)S(1)} %bitcast.224, f32[256,2,256]{2,1,0:T(2,128)S(1)} %bitcast.214), kind=kCustom, calls=%fused_computation.2 | custom fusion | bytes 1573888 | tf_op jit(solution)/shard_map/scatter | solution.py:73
  44.8 3.5 all-to-all-start.1
  48.4 4.2 broadcast_multiply_fusion.1
  52.7 4.5 all-to-all-done.1
  57.2 30.9 %scatter_fusion.1 = f32[2560,2,256]{2,1,0:T(2,128)} fusion(f32[2560,2,256]{2,1,0:T(2,128)} %broadcast_multiply_fusion.1, s32[256]{0:T(256)S(1)} %bitcast.225, f32[256,2,256]{2,1,0:T(2,128)S(1)} %bitcast.213), kind=kCustom, calls=%fused_computation.3 | custom fusion | flops 131072 | bytes 1573888 | tf_op jit(solution)/shard_map/scatter-add | solution.py:95
  88.1 8.8 %copy.88 = f32[2560,2,256]{0,2,1:T(8,128)} copy(f32[2560,2,256]{2,1,0:T(2,128)} %scatter_fusion.1) | data formatting | bytes 10485760 | tf_op jit(solution)/shard_map/scatter-add | solution.py:95
  97.0 1.0 fusion.18
  98.0 1.0 pad_maximum_fusion.3
  99.7 9.7 %copy.100 = bf16[10,1,256,5,1,256]{2,5,3,0,4,1:T(8,128)(2,1)} copy(bf16[10,1,256,5,1,256]{5,2,4,3,1,0:T(8,128)(2,1)} %param.11) | data formatting | bytes 13107200 | tf_op args[0]
  109.9 0.8 copy.99
  110.7 258.1 %all-reduce.4.cloned.1.call-done = f32[2560,2,256]{0,2,1:T(8,128)} async-done(((f32[2560,2,256]{0,2,1:T(8,128)}), f32[2560,2,256]{0,2,1:T(8,128)}) %all-reduce.4.cloned.1.call-update) | async-done | bytes 5242896 | tf_op jit(solution)/shard_map/psum | solution.py:115
  368.8 3.0 broadcast_multiply_fusion
  371.8 2.3 copy-done.1
  374.1 1.6 slice_bitcast_fusion.1
  375.8 9.2 %reduce_sum.29 = f32[3,256,256]{2,1,0:T(8,128)S(1)} reduce(f32[32,3,256,256]{3,2,1,0:T(8,128)} %bitcast.212, f32[]{:T(128)} %constant.211.clone.1), dimensions={0}, to_apply=%region_0.0 | reduce | flops 6094848 | bytes 25952260 | tf_op jit(solution)/shard_map/reduce_sum | solution.py:104
  386.5 4.8 gather_fusion
  391.6 11.7 %cholesky.130 = f32[128,128]{1,0:T(8,128)S(1)} custom-call(f32[128,128]{1,0:T(8,128)S(1)} %cholesky.194), custom_call_target="Cholesky" | custom-call | tf_op jit(solution)/shard_map/jit(cholesky)/cholesky | solution.py:31
  403.4 9.8 %custom-call.20 = f32[1,128,128]{1,2,0:T(8,128)S(1)} custom-call(f32[1,128,128]{2,1,0:T(8,128)S(1)} %get-tuple-element.87), custom_call_target="InvertDiagBlocksLowerTriangular" | custom-call | tf_op jit(solution)/shard_map/jit(cholesky)/cholesky | solution.py:31
  413.7 11.7 %cholesky.147 = f32[128,128]{1,0:T(8,128)S(1)} custom-call(f32[128,128]{1,0:T(8,128)S(1)} %convolution_subtract_fusion.6), custom_call_target="Cholesky" | custom-call | tf_op jit(solution)/shard_map/jit(cholesky)/cholesky | solution.py:31
  425.5 0.7 compare_reduce_fusion.2
  427.6 4.1 while.6
  428.2 1.4 bitcast_dynamic-update-slice_fusion.4
  430.3 1.4 bitcast_dynamic-update-slice_fusion.4
  431.7 20.1 %custom-call.21 = f32[2,128,128]{1,2,0:T(8,128)S(1)} custom-call(f32[2,128,128]{2,1,0:T(8,128)S(1)} %get-tuple-element.41), custom_call_target="InvertDiagBlocksLowerTriangular" | custom-call | tf_op jit(solution)/shard_map/jit(_solve_triangular)/triangular_solve | solution.py:17
  452.5 2.6 fusion.13
  455.0 2.6 convolution_subtract_fusion.2
  457.6 1.5 copy.90
  459.5 1.4 convolution_subtract_fusion.3
  460.9 2.2 fusion.42
  463.3 5.8 fusion.8
  469.3 0.7 copy-done.8
  470.0 11.9 %cholesky.164 = f32[128,128]{1,0:T(8,128)S(1)} custom-call(f32[128,128]{1,0:T(8,128)S(1)} %cholesky.197), custom_call_target="Cholesky" | custom-call | tf_op jit(solution)/shard_map/jit(cholesky)/cholesky | solution.py:34
  481.9 9.8 %custom-call.22 = f32[1,128,128]{1,2,0:T(8,128)S(1)} custom-call(f32[1,128,128]{2,1,0:T(8,128)S(1)} %get-tuple-element.83), custom_call_target="InvertDiagBlocksLowerTriangular" | custom-call | tf_op jit(solution)/shard_map/jit(cholesky)/cholesky | solution.py:34
  491.7 1.0 constant_dynamic-update-slice_fusion
  492.8 1.1 convolution_subtract_fusion.5
  493.9 11.7 %cholesky.181 = f32[128,128]{1,0:T(8,128)S(1)} custom-call(f32[128,128]{1,0:T(8,128)S(1)} %convolution_subtract_fusion.5), custom_call_target="Cholesky" | custom-call | tf_op jit(solution)/shard_map/jit(cholesky)/cholesky | solution.py:34
  508.1 1.0 select_bitcast_fusion
  509.1 3.8 while.7
  509.7 1.3 bitcast_dynamic-update-slice_fusion.5
  511.7 1.3 bitcast_dynamic-update-slice_fusion.5
  513.0 20.5 %custom-call.23 = f32[2,128,128]{1,2,0:T(8,128)} custom-call(f32[2,128,128]{2,1,0:T(8,128)S(1)} %get-tuple-element.42), custom_call_target="InvertDiagBlocksLowerTriangular" | custom-call | tf_op jit(solution)/shard_map/jit(_solve_triangular)/triangular_solve | solution.py:17
  533.5 2.7 fusion.11
  536.2 1.1 copy-done.3
  537.3 2.3 convolution_subtract_fusion.1
  539.6 2.8 copy.97
  542.4 3.7 fusion.34
  546.9 2.2 copy-done
  549.1 2.0 copy.107
  551.1 3.2 dot_general.16
  554.4 0.8 copy-done.10
  555.2 11.4 %convert_multiply_fusion = (f32[10,256,5,256]{1,3,2,0:T(8,128)}, f32[10,256,5,256]{1,3,2,0:T(8,128)}) fusion(bf16[10,1,256,5,1,256]{2,5,3,0,4,1:T(8,128)(2,1)} %copy.100, f32[10,5]{1,0:T(8,128)S(1)} %bitcast.217, pred[256,256]{0,1:T(8,128)(4,1)S(1)} %copy-done.10), kind=kLoop, calls=%fused_computation.8 | loop fusion | flops 9830400 | bytes 32833736 | tf_op jit(solution)/shard_map/mul | solution.py:145
  566.6 14.0 %copy.102 = f32[10,256,5,256]{3,1,2,0:T(8,128)} copy(f32[10,256,5,256]{1,3,2,0:T(8,128)} %get-tuple-element.67) | data formatting | bytes 26214400 | tf_op jit(solution)/shard_map/jit(tril)/select_n | solution.py:13
  580.6 14.2 %copy.105 = f32[10,256,5,256]{3,1,2,0:T(8,128)} copy(f32[10,256,5,256]{1,3,2,0:T(8,128)} %get-tuple-element.66) | data formatting | bytes 26214400 | tf_op jit(solution)/shard_map/mul | solution.py:145
  594.9 10.6 %copy.106 = f32[2560,2,256]{2,1,0:T(2,128)} copy(f32[2560,2,256]{2,0,1:T(8,128)} %copy-done) | data formatting | bytes 10485760 | tf_op jit(solution)/shard_map/scatter | solution.py:120
  605.6 8.0 %reshape.410 = f32[10,256,512,1]{2,1,0,3:T(8,128)} reshape(f32[2560,2,256]{2,1,0:T(2,128)} %copy.106) | data formatting | bytes 10485760 | tf_op jit(solution)/shard_map/dot_general | solution.py:128
  613.5 2.0 dynamic-slice_bitcast_fusion
  615.6 30.2 %fusion.6 = f32[10,1,256,5,1,256]{5,2,3,0,4,1:T(8,128)S(1)} fusion(f32[10,256,5,256]{3,1,2,0:T(8,128)} %copy.102, f32[10,256,5,256]{3,1,2,0:T(8,128)} %copy.105, bf16[10,1,256,5,1,256]{2,5,3,0,4,1:T(8,128)(2,1)} %copy.100, f32[10,256,256]{2,1,0:T(8,128)S(1)} %dynamic-slice_bitcast_fusion, pred[5]{0:T(512)(128)(4,1)S(1)} %broadcast_compare_fusion.3, ...), kind=kOutput, calls=%fused_computation.17 | convolution fusion | flops 20158873600 | bytes 56426652 | tf_op jit(solution)/shard_map/dot_general | solution.py:128
  645.8 15.0 %copy.108 = f32[10,1,256,5,1,256]{5,4,3,2,1,0:T(1,128)} copy(f32[10,1,256,5,1,256]{5,2,3,0,4,1:T(8,128)S(1)} %fusion.6) | data formatting | bytes 26214400 | tf_op jit(solution)/shard_map/reshape | solution.py:152
  (116 shorter events, 12.8 us)
Async XLA Ops:
  13.8 31.0 %all-to-all-start = ((f32[4,1,64]{2,1,0:T(1,128)}), f32[4,1,64]{2,1,0:T(1,128)S(1)}, u32[]{:S(2)}, u32[]{:S(2)}) async-start(f32[4,1,64]{2,1,0:T(1,128)} %all_to_all.9), calls=%async_computation | async-start | bytes 4096 | tf_op jit(solution)/shard_map/all_to_all | solution.py:88
  18.1 1.3 slice-start
  19.4 1.2 copy-start.9
  44.8 12.3 %all-to-all-start.1 = ((f32[4,64,2,256]{3,2,1,0:T(2,128)}), f32[4,64,2,256]{3,2,1,0:T(2,128)S(1)}, u32[]{:S(2)}, u32[]{:S(2)}) async-start(f32[4,64,2,256]{3,2,1,0:T(2,128)} %bitcast.27), calls=%async_computation.1 | async-start | bytes 1048576 | tf_op jit(solution)/shard_map/all_to_all | solution.py:81
  48.3 320.4 %all-reduce.4.cloned.1.call-start = ((), (), s32[]{:S(2)}) async-start(), calls=%async_computation.2 | async-start | bytes 10485760 | tf_op jit(solution)/shard_map/psum | solution.py:115
  96.9 2.2 copy-start.12
  96.9 278.9 %all-gather.3.cloned.1.call-start = ((), (), s32[]{:S(2)}) async-start(), calls=%async_computation.4 | async-start | bytes 25952256 | tf_op jit(solution)/shard_map/all_gather | solution.py:105
  99.0 516.6 %all-reduce.6.cloned.1.call-start = ((), (), s32[]{:S(2)}) async-start(), calls=%async_computation.3 | async-start | bytes 5242880 | tf_op jit(solution)/shard_map/psum | solution.py:9
  371.8 2.4 copy-start.1
  391.4 60.7 %copy-start.6 = (f32[512,512]{0,1:T(8,128)}, f32[512,512]{0,1:T(8,128)S(1)}, u32[]{:S(2)}) copy-start(f32[512,512]{0,1:T(8,128)S(1)} %select_add_fusion) | copy-start | bytes 3145732
  459.1 4.1 copy-start.2
  469.3 0.7 copy-start.8
  505.6 2.5 copy-start.7
  533.5 3.8 copy-start.4
  536.2 1.1 copy-start.3
  537.3 5.1 copy-start.11
  542.4 3.7 copy-start.5
  546.7 2.4 copy-start
  554.3 0.8 copy-start.10
Sparse Core Ops, SparseCore 0:
  97.0 271.6 all-reduce.3
  554.5 58.7 all-reduce.5
Sparse Core Ops, SparseCore 1:
  100.4 227.4 all-gather.2
